TPU v7x, 32 devices: a whole 2x2x4 slice. The times are simulated.
32 devices in a mesh: dp: 4 (over y, x), expert: 8 (over z, core).
Axes of the slice: x: 2, y: 2, z: 4, core: 2. Of those that a mesh axis runs over, the one named last changes fastest.
Arguments:
- tokens: bfloat16 [4096, 2048], P(('dp', 'expert')), may hold values from -6 to 6
- cotangent: bfloat16 [4096, 2048], P(('dp', 'expert')), may hold values from -6 to 6
- expert_ids: int32 [4096, 4], P(('dp', 'expert')), may hold values from 0 to 7, all different within a row; in each aligned block of 128 rows (0 to 127, 128 to 255, ...) at most 96 rows name the same one
- gate_probs: float32 [4096, 4], P(('dp', 'expert')), may hold values from 0.05 to 1
- up_weight: bfloat16 [8, 2048, 768], P('expert', None, 'dp'), may hold values from -0.125 to 0.125
- down_weight: float32 [8, 768, 2048], P('expert', 'dp'), may hold values from -28 to 28
- moment1: float32 [8, 768, 2048], P('expert', 'dp'), may hold values from -60 to 60
- moment2: float32 [8, 768, 2048], P('expert', 'dp'), may hold values from 0.05 to 5
- pair_match: int32 [8], replicated, may hold values from 0 to 7, as said below
Outputs:
- down_out: float32 [8, 768, 2048], P('expert', 'dp')
- moment1_out: float32 [8, 768, 2048], P('expert', 'dp')
- moment2_out: float32 [8, 768, 2048], P('expert', 'dp')
Inputs may be any that keep to these rules, and one draw needn't show every extreme that they name: `expert_ids`: each row names 4 different experts. Within the rows of one device (aligned blocks of 128 rows) no expert is named by more than 96 rows, a bound that some block reaches. A perfect matching: pair_match[pair_match[i]] = i and pair_match[i] != i for every i.
All inputs are finite; a program needn't handle non-finite values.
Results may differ from a plain program's by a relative error of at most 0.00035.
Values may be sent and summed in bfloat16 or wider, within the bound.
No kernel may reach another device: no remote copies, remote signals or barrier semaphores. Data moves between devices by JAX's collectives and lax.ppermute only.
A program may use at most 128 MiB of HBM per device.

v0:
```python
import jax
import jax.numpy as jnp
from jax import lax
from jax.sharding import PartitionSpec as P

beta_one = 0.9
beta_two = 0.999
epsilon = 1e-06
learn_rate = 0.05


def relocate(states, pair_match):
    group_size = lax.axis_size("expert")
    count_states = len(states)
    stacked = jnp.stack(states).reshape(count_states, group_size, -1)
    chosen = jnp.take(
        lax.all_to_all(stacked, "expert", split_axis=1, concat_axis=1, tiled=True),
        pair_match,
        axis=1,
    )
    arrived = lax.all_to_all(chosen, "expert", split_axis=1, concat_axis=1, tiled=True)
    arrived = arrived.reshape((count_states,) + states[0].shape)
    return tuple((arrived[index] for index in range(count_states)))


def expert_gradient(tokens, cotangent, expert_ids, gate_probs, up_weight):
    group_size = lax.axis_size("expert")
    tok_rows, top_count = expert_ids.shape
    width = tokens.shape[1]
    capacity = 3 * tok_rows * top_count // (2 * group_size)
    total = tok_rows * top_count
    flat_ids = expert_ids.reshape(-1)
    picked = (flat_ids[:, None] == jnp.arange(group_size, dtype=jnp.int32)[None, :]).astype(
        jnp.int32
    )
    ranking = jnp.sum((jnp.cumsum(picked, axis=0) - 1) * picked, axis=1)
    slot_index = flat_ids * capacity + ranking
    source = (
        jnp.full((group_size * capacity,), total, jnp.int32)
        .at[slot_index]
        .set(jnp.arange(total, dtype=jnp.int32))
    )
    filled = source < total
    safe_source = jnp.minimum(source, total - 1)
    row_index = safe_source // top_count
    weights_row = jnp.where(filled, gate_probs.reshape(-1)[safe_source], jnp.float32(0.0))
    sent_tokens = jnp.where(filled[:, None], tokens[row_index], jnp.zeros((), jnp.bfloat16))
    sent_scaled = (weights_row[:, None] * cotangent[row_index].astype(jnp.float32)).astype(
        jnp.bfloat16
    )
    sent_tokens = sent_tokens.reshape(group_size, capacity, width)
    sent_scaled = sent_scaled.reshape(group_size, capacity, width)
    got_tokens, got_scaled = (
        lax.all_to_all(sent_tokens, "expert", split_axis=0, concat_axis=0, tiled=True),
        lax.all_to_all(sent_scaled, "expert", split_axis=0, concat_axis=0, tiled=True),
    )
    rows_tokens = got_tokens.reshape(-1, width)
    rows_scaled = got_scaled.reshape(-1, width)
    hidden = jax.nn.silu(
        jnp.dot(
            rows_tokens,
            lax.all_gather(up_weight[0], "dp", axis=1, tiled=True),
            preferred_element_type=jnp.float32,
        )
    ).astype(jnp.bfloat16)
    return lax.psum_scatter(
        lax.dot_general(
            hidden, rows_scaled, (((0,), (0,)), ((), ())), preferred_element_type=jnp.float32
        ),
        "dp",
        scatter_dimension=0,
        tiled=True,
    )


def lamb_step(weight, moment_one, moment_two, gradient):
    first = beta_one * moment_one + (1.0 - beta_one) * gradient
    second = beta_two * moment_two + (1.0 - beta_two) * gradient * gradient
    update = first / (jnp.sqrt(second) + epsilon)
    weight_sq, update_sq = lax.psum((jnp.sum(weight * weight), jnp.sum(update * update)), "dp")
    trust_ratio = jnp.sqrt(weight_sq) / (jnp.sqrt(update_sq) + epsilon)
    renewed = weight - learn_rate * trust_ratio * update
    return (renewed, first, second)


def local(
    tokens, cotangent, expert_ids, gate_probs, up_weight, down_weight, moment1, moment2, pair_match
):
    gradient = expert_gradient(tokens, cotangent, expert_ids, gate_probs, up_weight)
    renewed, first, second = lamb_step(down_weight[0], moment1[0], moment2[0], gradient)
    renewed, first, second = relocate((renewed, first, second), pair_match)
    return (renewed[None], first[None], second[None])


def solution(mesh):
    in_specs = (
        P(("dp", "expert"), None),
        P(("dp", "expert"), None),
        P(("dp", "expert"), None),
        P(("dp", "expert"), None),
        P("expert", None, "dp"),
        P("expert", "dp", None),
        P("expert", "dp", None),
        P("expert", "dp", None),
        P(),
    )
    out_specs = (P("expert", "dp", None), P("expert", "dp", None), P("expert", "dp", None))
    return jax.shard_map(local, mesh=mesh, in_specs=in_specs, out_specs=out_specs, check_vma=False)
```

profile of v0, /device:TPU:0, one launch (start us, length us, event | category | flops | bytes accessed | tf_op | source)
XLA Modules:
  0.0 632.6 jit_solution(5432400970827513326)
XLA Ops:
  7.2 0.8 copy.13
  8.0 0.1 eq.29
  8.1 0.1 eq.25
  8.2 0.7 broadcast_multiply_fusion
  8.9 1.1 reduce-window.6
  10.1 0.2 slice_reduce_fusion.3
  10.3 0.1 copy.12
  10.4 0.1 mul.85
  10.6 0.1 fusion.10
  10.7 2.4 scatter_custom_fusion
  13.1 0.8 copy.15
  13.9 0.1 reshape.103
  14.0 5.0 gather_fusion.1
  19.1 0.1 broadcast_in_dim.42
  19.2 4.3 gather_fusion
  23.5 3.8 broadcast_select_fusion
  27.3 6.5 %all-to-all-start = ((bf16[8,96,2048]{2,1,0:T(8,128)(2,1)}), bf16[8,96,2048]{2,1,0:T(8,128)(2,1)}, u32[]{:S(2)}, u32[]{:S(2)}) async-start(bf16[8,96,2048]{2,1,0:T(8,128)(2,1)} %broadcast_select_fusion), calls=%async_computation | async-start | bytes 6291456 | tf_op jit(solution)/shard_map/all_to_all | solution.py:54
  33.8 0.1 mul.88
  33.9 4.2 gather_fusion.2
  38.1 4.2 fusion
  42.3 63.1 %all-to-all-done = bf16[8,96,2048]{2,1,0:T(8,128)(2,1)} async-done(((bf16[8,96,2048]{2,1,0:T(8,128)(2,1)}), bf16[8,96,2048]{2,1,0:T(8,128)(2,1)}, u32[]{:S(2)}, u32[]{:S(2)}) %all-to-all-start) | async-done | bytes 3145760 | tf_op jit(solution)/shard_map/all_to_all | solution.py:54
  105.4 4.4 all-to-all-start.1
  109.8 0.0 all-gather.3.cloned.1.call-start
  109.9 0.7 all-gather.3.cloned.1.call-update
  110.6 0.2 reduce-scatter.2.cloned.1.call-start
  110.8 46.9 %all-gather.3.cloned.1.call-done = bf16[1,2048,768]{1,2,0:T(8,128)(2,1)} async-done(((bf16[1,2048,192]{1,2,0:T(8,128)(2,1)}), bf16[1,2048,768]{1,2,0:T(8,128)(2,1)}) %all-gather.3.cloned.1.call-update) | async-done | bytes 3145744 | tf_op jit(solution)/shard_map/all_gather | solution.py:62
  157.7 23.6 %all-to-all-done.1 = bf16[8,96,2048]{2,1,0:T(8,128)(2,1)} async-done(((bf16[8,96,2048]{2,1,0:T(8,128)(2,1)}), bf16[8,96,2048]{2,1,0:T(8,128)(2,1)}, u32[]{:S(2)}, u32[]{:S(2)}) %all-to-all-start.1) | async-done | bytes 3145760 | tf_op jit(solution)/shard_map/all_to_all | solution.py:55
  181.3 16.3 %fusion.8 = f32[768,2048]{1,0:T(8,128)} fusion(bf16[768,2048]{1,0:T(8,128)(2,1)} %bitcast.10, bf16[768,2048]{1,0:T(8,128)(2,1)} %bitcast.7, bf16[1,2048,768]{1,2,0:T(8,128)(2,1)} %all-gather.3.cloned.1.call-done), kind=kOutput, calls=%fused_computation.24 | convolution fusion | flops 4834787328 | bytes 15728640 | tf_op jit(solution)/shard_map/dot_general | solution.py:67
  197.6 0.0 reduce-scatter.2.cloned.1.call-update
  197.6 1.4 copy-done.3
  199.0 1.0 fusion.6
  200.0 66.7 %reduce-scatter.2.cloned.1.call-done = f32[192,2048]{1,0:T(8,128)} async-done(((f32[768,2048]{1,0:T(8,128)}), f32[192,2048]{1,0:T(8,128)}) %reduce-scatter.2.cloned.1.call-update) | async-done | bytes 1572880 | tf_op jit(solution)/shard_map/reduce_scatter | solution.py:66
  266.8 5.0 multiply_reduce_fusion
  271.8 9.8 %all-reduce = (f32[]{:T(128)}, f32[]{:T(128)}) all-reduce(f32[]{:T(128)} %fusion.6, f32[]{:T(128)} %get-tuple-element.8), channel_id=1, replica_groups=mesh['dp'=4,'expert'=8] {'dp'}, use_global_device_ids=true, to_apply=%region_1.2 | all-reduce | flops 2 | bytes 16 | tf_op jit(solution)/shard_map/psum | solution.py:80
  282.9 2.8 stack.17
  285.7 4.2 stack.18
  290.0 3.7 bitcast_subtract_fusion
  293.7 4.4 stack.16
  298.0 7.5 %pad_maximum_fusion = f32[3,8,49152]{2,0,1:T(4,128)} fusion(f32[1,8,49152]{2,0,1:T(1,128)} %stack.18, f32[1,8,49152]{2,0,1:T(1,128)S(1)} %copy-done.4, f32[1,8,49152]{2,0,1:T(1,128)} %stack.16), kind=kLoop, calls=%fused_computation.5 | loop fusion | flops 2359296 | bytes 9437184 | tf_op jit(solution)/shard_map/stack | solution.py:15
  305.5 4.9 all-to-all-start.2
  310.5 138.9 %all-to-all-done.2 = f32[3,8,49152]{2,0,1:T(4,128)} async-done(((f32[3,8,49152]{2,0,1:T(4,128)}), f32[3,8,49152]{2,0,1:T(4,128)}, u32[]{:S(2)}, u32[]{:S(2)}) %all-to-all-start.2) | async-done | bytes 4718624 | tf_op jit(solution)/shard_map/all_to_all | solution.py:17
  449.3 9.4 %gather_fusion.3 = f32[8,3,49152]{2,1,0:T(4,128)} fusion(f32[3,8,49152]{2,0,1:T(4,128)} %all-to-all-done.2, s32[1024]{0:T(1024)S(1)} %pad_clamp_fusion), kind=kCustom, calls=%fused_computation.3 | custom fusion | bytes 9437216 | tf_op jit(solution)/shard_map/jit(_take)/gather | solution.py:16
  458.7 4.4 select_bitcast_fusion
  463.1 141.4 %all_to_all.20 = f32[3,8,49152]{2,0,1:T(4,128)S(1)} all-to-all(f32[3,8,49152]{2,0,1:T(4,128)S(1)} %select_bitcast_fusion), channel_id=1, replica_groups=mesh['dp'=4,'expert'=8] {'expert'}, dimensions={1} | all-to-all | bytes 9437184 | tf_op jit(solution)/shard_map/all_to_all | solution.py:21
  604.5 14.1 %slice_reduce_fusion = (f32[8,49152]{1,0:T(8,128)S(1)}, f32[8,49152]{1,0:T(8,128)}, f32[8,49152]{1,0:T(8,128)}) fusion(f32[3,8,49152]{2,0,1:T(4,128)S(1)} %all_to_all.20), kind=kLoop, calls=%fused_computation.15 | loop fusion | bytes 9437184 | tf_op jit(solution)/shard_map/slice | solution.py:23
  618.6 2.8 slice.27
  621.5 2.8 slice.29
  624.3 1.4 slice.31
  (22 shorter events, 0.1 us)
Async XLA Ops:
  7.2 12.0 %copy-start = (bf16[128,2048]{1,0:T(8,128)(2,1)S(1)}, bf16[128,2048]{1,0:T(8,128)(2,1)}, u32[]{:S(2)}) copy-start(bf16[128,2048]{1,0:T(8,128)(2,1)} %param.9) | copy-start | bytes 1572868
  27.3 6.6 %copy-start.2 = (bf16[128,2048]{1,0:T(8,128)(2,1)S(1)}, bf16[128,2048]{1,0:T(8,128)(2,1)}, u32[]{:S(2)}) copy-start(bf16[128,2048]{1,0:T(8,128)(2,1)} %param.10) | copy-start | bytes 1572868
  27.3 78.1 %all-to-all-start = ((bf16[8,96,2048]{2,1,0:T(8,128)(2,1)}), bf16[8,96,2048]{2,1,0:T(8,128)(2,1)}, u32[]{:S(2)}, u32[]{:S(2)}) async-start(bf16[8,96,2048]{2,1,0:T(8,128)(2,1)} %broadcast_select_fusion), calls=%async_computation | async-start | bytes 6291456 | tf_op jit(solution)/shard_map/all_to_all | solution.py:54
  105.4 76.0 %all-to-all-start.1 = ((bf16[8,96,2048]{2,1,0:T(8,128)(2,1)}), bf16[8,96,2048]{2,1,0:T(8,128)(2,1)}, u32[]{:S(2)}, u32[]{:S(2)}) async-start(bf16[8,96,2048]{2,1,0:T(8,128)(2,1)} %fusion), calls=%async_computation.1 | async-start | bytes 6291456 | tf_op jit(solution)/shard_map/all_to_all | solution.py:55
  109.8 47.9 %all-gather.3.cloned.1.call-start = ((), (), s32[]{:S(2)}) async-start(), calls=%async_computation.6 | async-start | bytes 3932160 | tf_op jit(solution)/shard_map/all_gather | solution.py:62
  110.6 156.2 %reduce-scatter.2.cloned.1.call-start = ((), (), s32[]{:S(2)}) async-start(), calls=%async_computation.5 | async-start | bytes 7864320 | tf_op jit(solution)/shard_map/reduce_scatter | solution.py:66
  197.6 1.4 copy-start.3
  293.7 4.4 copy-start.4
  305.5 4.9 copy-start.5
  305.5 143.8 %all-to-all-start.2 = ((f32[3,8,49152]{2,0,1:T(4,128)}), f32[3,8,49152]{2,0,1:T(4,128)}, u32[]{:S(2)}, u32[]{:S(2)}) async-start(f32[3,8,49152]{2,0,1:T(4,128)} %pad_maximum_fusion), calls=%async_computation.3 | async-start | bytes 12582912 | tf_op jit(solution)/shard_map/all_to_all | solution.py:17
  624.3 1.4 copy-start.1
Sparse Core Ops, SparseCore 0:
  112.5 45.1 all-gather.2
  197.8 68.9 reduce-scatter.1
where the time goes:
time: 633 us
  waiting for transfers between devices  340 us (54%)
  blocking collectives  151 us (24%)
  local copies, waits for them, and re-layouts  61.9 us (10%)
  other arithmetic  31.6 us (5%)
  matrix products  16.3 us (3%)
  starting transfers between devices  16.1 us (3%)
  between operations  15.6 us (2%)
    all_to_all x1, blocking collectives, relocate(): lax.all_to_all(chosen, 'expert', split_axis=1, concat_axis=1, tiled=True)  141 us
    all_to_all x1, waiting for transfers between devices, relocate(): lax.all_to_all(stacked, 'expert', split_axis=1, concat_axis=1, tiled=True)  139 us
    reduce_scatter x1, waiting for transfers between devices, expert_gradient(): lax.psum_scatter(lax.dot_general(hidden, rows_scaled, (((0,), (0,)), ((),...  66.7 us
    all_to_all x1, waiting for transfers between devices, expert_gradient(): lax.all_to_all(sent_tokens, 'expert', split_axis=0, concat_axis=0, tiled=...  63.1 us
    all_gather x1, waiting for transfers between devices, expert_gradient(): lax.all_gather(up_weight[0], 'dp', axis=1, tiled=True)  46.9 us
    all_to_all x1, waiting for transfers between devices, expert_gradient(): lax.all_to_all(sent_scaled, 'expert', split_axis=0, concat_axis=0, tiled=...  23.6 us
    slice x4, local copies, waits for them, and re-layouts, relocate(): return tuple((arrived[index] for index in range(count_states)))  21.2 us
    dot_general x1, matrix products, expert_gradient(): lax.dot_general(hidden, rows_scaled, (((0,), (0,)), ((), ())), preferred_...  16.3 us
  transfers between devices with their start and end apart: 5, of which 5 were waited for; matrix products, arithmetic and copies ran while one was open for 1% of the time, Pallas kernels for 0%

commit v1 on v0

--- a/solution.py
+++ b/solution.py
@@ -1,3 +1,4 @@
+import functools
 import jax
 import jax.numpy as jnp
 from jax import lax
@@ -7,6 +8,35 @@
 beta_two = 0.999
 epsilon = 1e-06
 learn_rate = 0.05
+
+
+def _render_members_all(arr_in, join_dim, vec):
+    u1, answer = (arr_in.shape[:join_dim], arr_in.shape[join_dim + 1 :])
+    return jnp.moveaxis(arr_in.reshape(*u1, vec, -1, *answer), join_dim, 0)
+
+
+def steps_all_push(mine, array_axis):
+    mine = jnp.moveaxis(mine, 0, array_axis)
+    earlier = mine.shape
+    return mine.reshape(
+        *earlier[:array_axis],
+        earlier[array_axis] * earlier[array_axis + 1],
+        *earlier[array_axis + 2 :]
+    )
+
+
+def name_gates(xin, ax_name, panel, raw):
+    n_now, block_now = (jax.lax.psum(1, ax_name), jax.lax.axis_index(ax_name))
+    val2 = _render_members_all(xin, panel, n_now)
+    kept_rows = [val2[block_now]]
+    for q in range(1, n_now):
+        z1 = val2[block_now ^ q]
+        kept_rows.append(jax.lax.ppermute(z1, ax_name, [(kk, kk ^ q) for kk in range(n_now)]))
+    val2 = jnp.stack(kept_rows)[block_now ^ jnp.arange(n_now)]
+    return steps_all_push(val2, raw)
+
+
+save_ratios = functools.partial(name_gates, ax_name="expert", panel=0, raw=0)
 
 
 def relocate(states, pair_match):
@@ -51,7 +81,7 @@
     sent_tokens = sent_tokens.reshape(group_size, capacity, width)
     sent_scaled = sent_scaled.reshape(group_size, capacity, width)
     got_tokens, got_scaled = (
-        lax.all_to_all(sent_tokens, "expert", split_axis=0, concat_axis=0, tiled=True),
+        save_ratios(sent_tokens),
         lax.all_to_all(sent_scaled, "expert", split_axis=0, concat_axis=0, tiled=True),
     )
     rows_tokens = got_tokens.reshape(-1, width)

time: 633 us -> 629 us (level)
  waiting for transfers between devices: 340 us -> 320 us
  local copies, waits for them, and re-layouts: 61.9 us -> 72.7 us
    ppermute x0 -> x7, waiting for transfers between devices: none -> 99 us  [name_gates(): jax.lax.ppermute(z1, ax_name, [(kk, kk ^ q) for kk in range(n_now)])]
    all_to_all x1 -> x0, waiting for transfers between devices: 63.1 us -> none  [expert_gradient(): lax.all_to_all(sent_tokens, 'expert', split_axis=0, concat_axis=0, tiled=...]
    all_gather x1, waiting for transfers between devices: 46.9 us -> 0.01 us  [expert_gradient(): lax.all_gather(up_weight[0], 'dp', axis=1, tiled=True)]
    all_to_all x1, waiting for transfers between devices: 23.6 us -> 0.01 us  [expert_gradient(): lax.all_to_all(sent_scaled, 'expert', split_axis=0, concat_axis=0, tiled=...]
    reduce_scatter x1, waiting for transfers between devices: 66.7 us -> 81.7 us  [expert_gradient(): lax.psum_scatter(lax.dot_general(hidden, rows_scaled, (((0,), (0,)), ((),...]
    ppermute x0 -> x7, starting transfers between devices: none -> 10.8 us  [name_gates(): jax.lax.ppermute(z1, ax_name, [(kk, kk ^ q) for kk in range(n_now)])]
    all_to_all x1 -> x0, starting transfers between devices: 6.49 us -> none  [expert_gradient(): lax.all_to_all(sent_tokens, 'expert', split_axis=0, concat_axis=0, tiled=...]
  transfers between devices with their start and end apart: 5 -> 11, of which waited for: 5 -> 6; matrix products, arithmetic and copies ran while one was open for 1% -> 3% of each run, Pallas kernels for 0% -> 0%
where the time goes in v1:
time: 629 us; the launch traced here: 628 us
  waiting for transfers between devices  320 us (51%)
  blocking collectives  151 us (24%)
  local copies, waits for them, and re-layouts  72.7 us (12%)
  other arithmetic  29.9 us (5%)
  starting transfers between devices  22.4 us (4%)
  matrix products  16.3 us (3%)
  between operations  15.7 us (2%)
    all_to_all x1, blocking collectives, relocate(): lax.all_to_all(chosen, 'expert', split_axis=1, concat_axis=1, tiled=True)  141 us
    all_to_all x1, waiting for transfers between devices, relocate(): lax.all_to_all(stacked, 'expert', split_axis=1, concat_axis=1, tiled=True)  139 us
    ppermute x7, waiting for transfers between devices, name_gates(): jax.lax.ppermute(z1, ax_name, [(kk, kk ^ q) for kk in range(n_now)])  99 us
    reduce_scatter x1, waiting for transfers between devices, expert_gradient(): lax.psum_scatter(lax.dot_general(hidden, rows_scaled, (((0,), (0,)), ((),...  81.7 us
    slice x4, local copies, waits for them, and re-layouts, relocate(): return tuple((arrived[index] for index in range(count_states)))  21.2 us
    dot_general x1, matrix products, expert_gradient(): lax.dot_general(hidden, rows_scaled, (((0,), (0,)), ((), ())), preferred_...  16.3 us
  transfers between devices with their start and end apart: 11, of which 6 were waited for; matrix products, arithmetic and copies ran while one was open for 3% of the time, Pallas kernels for 0%

profile of v1, /device:TPU:0, one launch (start us, length us, event | category | flops | bytes accessed | tf_op | source)
XLA Modules:
  0.0 628.5 jit_solution(11384201023638721064)
XLA Ops:
  7.2 0.8 copy.13
  8.2 0.7 broadcast_multiply_fusion
  8.9 1.1 reduce-window.6
  10.7 2.4 scatter_custom_fusion
  13.1 0.8 copy.15
  14.0 5.0 gather_fusion.2
  19.1 4.3 gather_fusion.3
  23.4 4.1 fusion
  27.6 6.5 %all-to-all-start = ((bf16[8,96,2048]{2,1,0:T(8,128)(2,1)}), bf16[8,96,2048]{2,1,0:T(8,128)(2,1)}, u32[]{:S(2)}, u32[]{:S(2)}) async-start(bf16[8,96,2048]{2,1,0:T(8,128)(2,1)} %fusion), calls=%async_computation | async-start | bytes 6291456 | tf_op jit(solution)/shard_map/all_to_all | solution.py:85
  35.1 4.3 gather_fusion
  39.4 2.2 broadcast_select_fusion
  41.6 1.0 dynamic-slice_bitcast_fusion
  43.1 1.6 collective-permute-start.1
  44.7 2.6 collective-permute-start.3
  47.5 3.5 collective-permute-start.5
  51.0 0.8 bitcast_dynamic-update-slice_fusion.6
  51.8 42.6 %collective-permute-done.1 = bf16[1,96,2048]{2,1,0:T(8,128)(2,1)S(1)} collective-permute-done((bf16[1,96,2048]{2,1,0:T(8,128)(2,1)S(1)}, bf16[1,96,2048]{2,1,0:T(8,128)(2,1)S(1)}, u32[]{:S(2)}, u32[]{:S(2)}) %collective-permute-start.1) | collective-permute-done | bytes 393248 | tf_op jit(solution)/shard_map/ppermute | solution.py:34
  94.4 2.4 collective-permute-start.6
  96.8 0.8 bitcast_dynamic-update-slice_fusion.5
  97.6 5.2 collective-permute-done.2
  102.8 0.8 bitcast_dynamic-update-slice_fusion.4
  103.6 44.7 %collective-permute-done.3 = bf16[1,96,2048]{2,1,0:T(8,128)(2,1)S(1)} collective-permute-done((bf16[1,96,2048]{2,1,0:T(8,128)(2,1)S(1)}, bf16[1,96,2048]{2,1,0:T(8,128)(2,1)S(1)}, u32[]{:S(2)}, u32[]{:S(2)}) %collective-permute-start.3) | collective-permute-done | bytes 393248 | tf_op jit(solution)/shard_map/ppermute | solution.py:34
  148.3 0.8 bitcast_dynamic-update-slice_fusion.3
  149.1 6.5 %collective-permute-done.4 = bf16[1,96,2048]{2,1,0:T(8,128)(2,1)S(1)} collective-permute-done((bf16[1,96,2048]{2,1,0:T(8,128)(2,1)S(1)}, bf16[1,96,2048]{2,1,0:T(8,128)(2,1)S(1)}, u32[]{:S(2)}, u32[]{:S(2)}) %collective-permute-start.4) | collective-permute-done | bytes 393248 | tf_op jit(solution)/shard_map/ppermute | solution.py:34
  155.5 0.8 bitcast_dynamic-update-slice_fusion.2
  156.3 0.8 bitcast_dynamic-update-slice_fusion.1
  157.1 0.8 bitcast_dynamic-update-slice_fusion
  157.9 4.3 gather_fusion.1
  162.2 16.3 %fusion.8 = f32[768,2048]{1,0:T(8,128)} fusion(bf16[768,2048]{1,0:T(8,128)(2,1)} %bitcast.26, bf16[768,2048]{1,0:T(8,128)(2,1)} %bitcast.68, bf16[1,2048,768]{1,2,0:T(8,128)(2,1)} %all-gather.3.cloned.1.call-done), kind=kOutput, calls=%fused_computation.25 | convolution fusion | flops 4834787328 | bytes 15728640 | tf_op jit(solution)/shard_map/dot_general | solution.py:97
  178.5 1.4 copy-done.3
  179.9 1.0 fusion.6
  180.9 81.7 %reduce-scatter.2.cloned.1.call-done = f32[192,2048]{1,0:T(8,128)} async-done(((f32[768,2048]{1,0:T(8,128)}), f32[192,2048]{1,0:T(8,128)}) %reduce-scatter.2.cloned.1.call-update) | async-done | bytes 1572880 | tf_op jit(solution)/shard_map/reduce_scatter | solution.py:96
  262.6 5.0 multiply_reduce_fusion
  267.6 9.8 %all-reduce = (f32[]{:T(128)}, f32[]{:T(128)}) all-reduce(f32[]{:T(128)} %fusion.6, f32[]{:T(128)} %get-tuple-element.8), channel_id=1, replica_groups=mesh['dp'=4,'expert'=8] {'dp'}, use_global_device_ids=true, to_apply=%region_1.2 | all-reduce | flops 2 | bytes 16 | tf_op jit(solution)/shard_map/psum | solution.py:110
  278.8 2.8 stack.49
  281.6 4.2 stack.50
  285.8 3.7 bitcast_subtract_fusion
  289.5 4.4 stack.48
  293.9 7.5 %pad_maximum_fusion = f32[3,8,49152]{2,0,1:T(4,128)} fusion(f32[1,8,49152]{2,0,1:T(1,128)} %stack.50, f32[1,8,49152]{2,0,1:T(1,128)S(1)} %copy-done.4, f32[1,8,49152]{2,0,1:T(1,128)} %stack.48), kind=kLoop, calls=%fused_computation.6 | loop fusion | flops 2359296 | bytes 9437184 | tf_op jit(solution)/shard_map/stack | solution.py:45
  301.4 4.9 all-to-all-start.1
  306.3 138.9 %all-to-all-done.1 = f32[3,8,49152]{2,0,1:T(4,128)} async-done(((f32[3,8,49152]{2,0,1:T(4,128)}), f32[3,8,49152]{2,0,1:T(4,128)}, u32[]{:S(2)}, u32[]{:S(2)}) %all-to-all-start.1) | async-done | bytes 4718624 | tf_op jit(solution)/shard_map/all_to_all | solution.py:47
  445.2 9.4 %gather_fusion.4 = f32[8,3,49152]{2,1,0:T(4,128)} fusion(f32[3,8,49152]{2,0,1:T(4,128)} %all-to-all-done.1, s32[1024]{0:T(1024)S(1)} %pad_clamp_fusion), kind=kCustom, calls=%fused_computation.4 | custom fusion | bytes 9437216 | tf_op jit(solution)/shard_map/jit(_take)/gather | solution.py:46
  454.5 4.4 select_bitcast_fusion
  458.9 141.4 %all_to_all.15 = f32[3,8,49152]{2,0,1:T(4,128)S(1)} all-to-all(f32[3,8,49152]{2,0,1:T(4,128)S(1)} %select_bitcast_fusion), channel_id=1, replica_groups=mesh['dp'=4,'expert'=8] {'expert'}, dimensions={1} | all-to-all | bytes 9437184 | tf_op jit(solution)/shard_map/all_to_all | solution.py:51
  600.4 14.1 %slice_reduce_fusion = (f32[8,49152]{1,0:T(8,128)S(1)}, f32[8,49152]{1,0:T(8,128)}, f32[8,49152]{1,0:T(8,128)}) fusion(f32[3,8,49152]{2,0,1:T(4,128)S(1)} %all_to_all.15), kind=kLoop, calls=%fused_computation.16 | loop fusion | bytes 9437184 | tf_op jit(solution)/shard_map/slice | solution.py:53
  614.5 2.8 slice.27
  617.3 2.9 slice.29
  620.2 1.4 slice.31
  (45 shorter events, 2.7 us)
Async XLA Ops:
  7.2 12.0 %copy-start = (bf16[128,2048]{1,0:T(8,128)(2,1)S(1)}, bf16[128,2048]{1,0:T(8,128)(2,1)}, u32[]{:S(2)}) copy-start(bf16[128,2048]{1,0:T(8,128)(2,1)} %param.10) | copy-start | bytes 1572868
  27.6 7.6 %copy-start.2 = (bf16[128,2048]{1,0:T(8,128)(2,1)S(1)}, bf16[128,2048]{1,0:T(8,128)(2,1)}, u32[]{:S(2)}) copy-start(bf16[128,2048]{1,0:T(8,128)(2,1)} %param.9) | copy-start | bytes 1572868
  27.6 134.7 %all-to-all-start = ((bf16[8,96,2048]{2,1,0:T(8,128)(2,1)}), bf16[8,96,2048]{2,1,0:T(8,128)(2,1)}, u32[]{:S(2)}, u32[]{:S(2)}) async-start(bf16[8,96,2048]{2,1,0:T(8,128)(2,1)} %fusion), calls=%async_computation | async-start | bytes 6291456 | tf_op jit(solution)/shard_map/all_to_all | solution.py:85
  34.1 128.2 %all-gather.3.cloned.1.call-start = ((), (), s32[]{:S(2)}) async-start(), calls=%async_computation.5 | async-start | bytes 3932160 | tf_op jit(solution)/shard_map/all_gather | solution.py:92
  34.8 227.8 %reduce-scatter.2.cloned.1.call-start = ((), (), s32[]{:S(2)}) async-start(), calls=%async_computation.4 | async-start | bytes 7864320 | tf_op jit(solution)/shard_map/reduce_scatter | solution.py:96
  42.6 4.9 collective-permute-start
  43.1 51.3 %collective-permute-start.1 = (bf16[1,96,2048]{2,1,0:T(8,128)(2,1)S(1)}, bf16[1,96,2048]{2,1,0:T(8,128)(2,1)S(1)}, u32[]{:S(2)}, u32[]{:S(2)}) collective-permute-start(bf16[1,96,2048]{2,1,0:T(8,128)(2,1)S(1)} %get-tuple-element.18), channel_id=1, source_target_pairs={{0,2},{1,3},{2,0},{3,1},{4,6},{5,7},{6,4},{7,5},{8,10},{9,11},{10,... | collective-permute-start | bytes 1179656 | tf_op jit(solution)/shard_map/ppermute | solution.py:34
  44.7 58.1 %collective-permute-start.2 = (bf16[1,96,2048]{2,1,0:T(8,128)(2,1)S(1)}, bf16[1,96,2048]{2,1,0:T(8,128)(2,1)S(1)}, u32[]{:S(2)}, u32[]{:S(2)}) collective-permute-start(bf16[1,96,2048]{2,1,0:T(8,128)(2,1)S(1)} %get-tuple-element.17), channel_id=1, source_target_pairs={{0,3},{1,2},{2,1},{3,0},{4,7},{5,6},{6,5},{7,4},{8,11},{9,10},{10,... | collective-permute-start | bytes 1179656 | tf_op jit(solution)/shard_map/ppermute | solution.py:34
  44.7 103.5 %collective-permute-start.3 = (bf16[1,96,2048]{2,1,0:T(8,128)(2,1)S(1)}, bf16[1,96,2048]{2,1,0:T(8,128)(2,1)S(1)}, u32[]{:S(2)}, u32[]{:S(2)}) collective-permute-start(bf16[1,96,2048]{2,1,0:T(8,128)(2,1)S(1)} %get-tuple-element.16), channel_id=1, source_target_pairs={{0,4},{1,5},{2,6},{3,7},{4,0},{5,1},{6,2},{7,3},{8,12},{9,13},{10,... | collective-permute-start | bytes 1179656 | tf_op jit(solution)/shard_map/ppermute | solution.py:34
  47.4 108.2 %collective-permute-start.4 = (bf16[1,96,2048]{2,1,0:T(8,128)(2,1)S(1)}, bf16[1,96,2048]{2,1,0:T(8,128)(2,1)S(1)}, u32[]{:S(2)}, u32[]{:S(2)}) collective-permute-start(bf16[1,96,2048]{2,1,0:T(8,128)(2,1)S(1)} %get-tuple-element.15), channel_id=1, source_target_pairs={{0,5},{1,4},{2,7},{3,6},{4,1},{5,0},{6,3},{7,2},{8,13},{9,12},{10,... | collective-permute-start | bytes 1179656 | tf_op jit(solution)/shard_map/ppermute | solution.py:34
  47.5 108.8 %collective-permute-start.5 = (bf16[1,96,2048]{2,1,0:T(8,128)(2,1)S(1)}, bf16[1,96,2048]{2,1,0:T(8,128)(2,1)S(1)}, u32[]{:S(2)}, u32[]{:S(2)}) collective-permute-start(bf16[1,96,2048]{2,1,0:T(8,128)(2,1)S(1)} %get-tuple-element.14), channel_id=1, source_target_pairs={{0,6},{1,7},{2,4},{3,5},{4,2},{5,3},{6,0},{7,1},{8,14},{9,15},{10,... | collective-permute-start | bytes 1179656 | tf_op jit(solution)/shard_map/ppermute | solution.py:34
  94.4 62.8 %collective-permute-start.6 = (bf16[1,96,2048]{2,1,0:T(8,128)(2,1)S(1)}, bf16[1,96,2048]{2,1,0:T(8,128)(2,1)S(1)}, u32[]{:S(2)}, u32[]{:S(2)}) collective-permute-start(bf16[1,96,2048]{2,1,0:T(8,128)(2,1)S(1)} %get-tuple-element.13), channel_id=1, source_target_pairs={{0,7},{1,6},{2,5},{3,4},{4,3},{5,2},{6,1},{7,0},{8,15},{9,14},{10,... | collective-permute-start | bytes 1179656 | tf_op jit(solution)/shard_map/ppermute | solution.py:34
  178.5 1.4 copy-start.3
  289.5 4.4 copy-start.4
  301.4 4.9 copy-start.5
  301.4 143.8 %all-to-all-start.1 = ((f32[3,8,49152]{2,0,1:T(4,128)}), f32[3,8,49152]{2,0,1:T(4,128)}, u32[]{:S(2)}, u32[]{:S(2)}) async-start(f32[3,8,49152]{2,0,1:T(4,128)} %pad_maximum_fusion), calls=%async_computation.2 | async-start | bytes 12582912 | tf_op jit(solution)/shard_map/all_to_all | solution.py:47
  617.3 4.3 copy-start.1
Sparse Core Ops, SparseCore 0:
  36.7 45.2 all-gather.2
  178.7 83.8 reduce-scatter.1
